TPU v7x, 512 devices: a whole 4x8x8 slice. The times are simulated.
512 devices in a mesh: region: 8 (over z), sub: 64 (over y, x, core).
Axes of the slice: x: 4, y: 8, z: 8, core: 2. Of those that a mesh axis runs over, the one named last changes fastest.
Arguments:
- right_side: bfloat16 [8, 64, 1024, 256], P('region', 'sub'), may hold values from -6 to 6
- local_inverse: bfloat16 [8, 64, 1024, 1024], P('region', 'sub')
- coupling: bfloat16 [8, 64, 4, 256, 256], P('region', 'sub'), may hold values from -0.75 to 0.75
- margin_blocks: int32 [4, 8, 64, 2], P(None, 'region', 'sub'), may hold values from 0 to 7, as said below
- partner: int32 [4, 512], replicated, may hold values from 0 to 511, as said below
- restriction: bfloat16 [8, 64, 64, 1024], P('region', 'sub'), may hold values from -0.375 to 0.375
- coarse_rows: bfloat16 [8, 4096, 4096], P('region', 'sub')
Outputs:
- solution: bfloat16 [8, 64, 1024, 256], P('region', 'sub')
Inputs may be any that keep to these rules, and one draw needn't show every extreme that they name: `margin_blocks`: for each colour, subdomain and k, a block number below 8; the 2 numbers of one colour and subdomain are distinct. For each colour a perfect matching of all subdomains: the partner of a subdomain's partner is the subdomain itself, and no subdomain is its own partner.
All inputs are finite; a program needn't handle non-finite values.
Results may differ from a plain program's by a relative error of at most 0.0052.
Values may be sent and summed in bfloat16 or wider, within the bound.
No kernel may reach another device: no remote copies, remote signals or barrier semaphores. Data moves between devices by JAX's collectives and lax.ppermute only.
A program may use at most 64 MiB of HBM per device.

v0:
```python
import jax
import jax.numpy as jnp
from jax import lax
from jax.sharding import PartitionSpec as P

BLK = 128
OVL_BLK = 2
COLORS = 4


def shards(right_side, local_inverse, coupling, margin_blocks, partner, restriction, coarse_rows):
    inverse = local_inverse[0, 0]
    tile_set = coupling[0, 0]
    own_blocks = margin_blocks[:, 0, 0, :]
    row_count = inverse.shape[0]
    columns = right_side.shape[-1]
    block_count = row_count // BLK
    span_rows = tile_set.shape[-1]
    sub_peers = lax.axis_size("sub")
    region_peers = lax.axis_size("region")
    all_peers = sub_peers * region_peers
    piece_len = span_rows * columns // all_peers
    residual = right_side[0, 0].astype(jnp.float32)
    accumulated = jnp.zeros(residual.shape, jnp.float32)
    block_ids = jnp.arange(block_count, dtype=jnp.int32)
    for colour in range(COLORS):
        picked = own_blocks[colour]
        tiled = residual.reshape(block_count, BLK, columns)
        sent_rows = jnp.take(tiled, picked, axis=0).reshape(span_rows, columns).astype(jnp.bfloat16)
        pieces = sent_rows.reshape(region_peers, sub_peers, piece_len)
        relayed = lax.all_to_all(
            lax.all_to_all(pieces, "region", split_axis=0, concat_axis=0, tiled=True),
            "sub",
            split_axis=1,
            concat_axis=1,
            tiled=True,
        )
        relayed = jnp.take(relayed.reshape(all_peers, piece_len), partner[colour], axis=0)
        returned = lax.all_to_all(
            lax.all_to_all(
                relayed.reshape(region_peers, sub_peers, piece_len),
                "region",
                split_axis=0,
                concat_axis=0,
                tiled=True,
            ),
            "sub",
            split_axis=1,
            concat_axis=1,
            tiled=True,
        )
        received = returned.reshape(span_rows, columns)
        coupled = jnp.dot(tile_set[colour], received, preferred_element_type=jnp.float32)
        one_hot = (picked[:, None] == block_ids[None, :]).astype(jnp.float32)
        added = jnp.einsum(
            "kb,kin->bin",
            one_hot,
            coupled.reshape(OVL_BLK, BLK, columns),
            precision=lax.Precision.HIGHEST,
        )
        widened = residual + added.reshape(row_count, columns)
        shaped = widened.astype(jnp.bfloat16)
        correction = jnp.dot(inverse, shaped, preferred_element_type=jnp.float32)
        accumulated = accumulated + correction
        residual = widened - 0.25 * correction
    settled = residual.astype(jnp.bfloat16)
    own_restriction = restriction[0, 0]
    projected = jnp.dot(own_restriction, settled, preferred_element_type=jnp.float32).astype(
        jnp.bfloat16
    )
    own_rows = coarse_rows[0]
    coarse = jnp.dot(
        own_rows,
        lax.all_gather(projected, "sub", axis=0, tiled=True),
        preferred_element_type=jnp.float32,
    ).astype(jnp.bfloat16)
    lifted = lax.dot_general(
        own_restriction, coarse, (((0,), (0,)), ((), ())), preferred_element_type=jnp.float32
    )
    return (accumulated + lifted).astype(jnp.bfloat16)[None, None]


def solution(mesh):
    placed = (
        P("region", "sub", None, None),
        P("region", "sub", None, None),
        P("region", "sub", None, None, None),
        P(None, "region", "sub", None),
        P(),
        P("region", "sub", None, None),
        P("region", "sub", None),
    )
    return jax.shard_map(
        shards,
        mesh=mesh,
        in_specs=placed,
        out_specs=P("region", "sub", None, None),
        check_vma=False,
    )
```

profile of v0, /device:TPU:1, one launch (start us, length us, event | category | flops | bytes accessed | tf_op | source)
XLA Modules:
  0.0 384.2 jit_solution(11332730340993844676)
XLA Ops:
  12.3 10.9 %all-to-all-start = ((bf16[8,64,128]{2,1,0:T(8,128)(2,1)}), bf16[8,64,128]{2,1,0:T(8,128)(2,1)S(1)}, u32[]{:S(2)}, u32[]{:S(2)}) async-start(bf16[8,64,128]{2,1,0:T(8,128)(2,1)} %convert_element_type.77), calls=%async_computation | async-start | bytes 262144 | tf_op jit(solution)/shard_map/all_to_all | solution.py:32
  23.2 7.7 %all-to-all-done = bf16[8,64,128]{2,1,0:T(8,128)(2,1)S(1)} async-done(((bf16[8,64,128]{2,1,0:T(8,128)(2,1)}), bf16[8,64,128]{2,1,0:T(8,128)(2,1)S(1)}, u32[]{:S(2)}, u32[]{:S(2)}) %all-to-all-start) | async-done | bytes 131104 | tf_op jit(solution)/shard_map/all_to_all | solution.py:32
  31.7 12.4 %all-to-all-start.1 = ((bf16[8,64,128]{2,0,1:T(8,128)(2,1)}), bf16[8,64,128]{2,0,1:T(8,128)(2,1)S(1)}, u32[]{:S(2)}, u32[]{:S(2)}) async-start(bf16[8,64,128]{2,0,1:T(8,128)(2,1)} %copy.98), calls=%async_computation.1 | async-start | bytes 262144 | tf_op jit(solution)/shard_map/all_to_all | solution.py:31
  44.1 11.1 %all-to-all-done.1 = bf16[8,64,128]{2,0,1:T(8,128)(2,1)S(1)} async-done(((bf16[8,64,128]{2,0,1:T(8,128)(2,1)}), bf16[8,64,128]{2,0,1:T(8,128)(2,1)S(1)}, u32[]{:S(2)}, u32[]{:S(2)}) %all-to-all-start.1) | async-done | bytes 131104 | tf_op jit(solution)/shard_map/all_to_all | solution.py:31
  56.7 10.7 %all_to_all.80 = bf16[8,64,128]{2,1,0:T(8,128)(2,1)S(1)} all-to-all(bf16[8,64,128]{2,1,0:T(8,128)(2,1)S(1)} %bitcast.164), channel_id=1, replica_groups=mesh['region'=8,'sub'=64] {'region'}, dimensions={0} | all-to-all | bytes 262144 | tf_op jit(solution)/shard_map/all_to_all | solution.py:40
  73.9 11.3 %all-to-all-done.3 = bf16[8,64,128]{2,0,1:T(8,128)(2,1)S(1)} async-done(((bf16[8,64,128]{2,0,1:T(8,128)(2,1)}), bf16[8,64,128]{2,0,1:T(8,128)(2,1)S(1)}, u32[]{:S(2)}, u32[]{:S(2)}) %all-to-all-start.3) | async-done | bytes 131104 | tf_op jit(solution)/shard_map/all_to_all | solution.py:39
  100.4 8.1 %all-to-all-done.4 = bf16[8,64,128]{2,1,0:T(8,128)(2,1)S(1)} async-done(((bf16[8,64,128]{2,1,0:T(8,128)(2,1)}), bf16[8,64,128]{2,1,0:T(8,128)(2,1)S(1)}, u32[]{:S(2)}, u32[]{:S(2)}) %all-to-all-start.4) | async-done | bytes 131104 | tf_op jit(solution)/shard_map/all_to_all | solution.py:32
  109.3 5.8 %all-to-all-start.5 = ((bf16[8,64,128]{2,0,1:T(8,128)(2,1)}), bf16[8,64,128]{2,0,1:T(8,128)(2,1)S(1)}, u32[]{:S(2)}, u32[]{:S(2)}) async-start(bf16[8,64,128]{2,0,1:T(8,128)(2,1)} %copy.108), calls=%async_computation.5 | async-start | bytes 262144 | tf_op jit(solution)/shard_map/all_to_all | solution.py:31
  115.1 11.3 %all-to-all-done.5 = bf16[8,64,128]{2,0,1:T(8,128)(2,1)S(1)} async-done(((bf16[8,64,128]{2,0,1:T(8,128)(2,1)}), bf16[8,64,128]{2,0,1:T(8,128)(2,1)S(1)}, u32[]{:S(2)}, u32[]{:S(2)}) %all-to-all-start.5) | async-done | bytes 131104 | tf_op jit(solution)/shard_map/all_to_all | solution.py:31
  132.0 8.1 %all-to-all-done.6 = bf16[8,64,128]{2,1,0:T(8,128)(2,1)S(1)} async-done(((bf16[8,64,128]{2,1,0:T(8,128)(2,1)}), bf16[8,64,128]{2,1,0:T(8,128)(2,1)S(1)}, u32[]{:S(2)}, u32[]{:S(2)}) %all-to-all-start.6) | async-done | bytes 131104 | tf_op jit(solution)/shard_map/all_to_all | solution.py:40
  140.9 5.8 %all-to-all-start.7 = ((bf16[8,64,128]{2,0,1:T(8,128)(2,1)}), bf16[8,64,128]{2,0,1:T(8,128)(2,1)S(1)}, u32[]{:S(2)}, u32[]{:S(2)}) async-start(bf16[8,64,128]{2,0,1:T(8,128)(2,1)} %copy.110), calls=%async_computation.7 | async-start | bytes 262144 | tf_op jit(solution)/shard_map/all_to_all | solution.py:39
  146.8 11.3 %all-to-all-done.7 = bf16[8,64,128]{2,0,1:T(8,128)(2,1)S(1)} async-done(((bf16[8,64,128]{2,0,1:T(8,128)(2,1)}), bf16[8,64,128]{2,0,1:T(8,128)(2,1)S(1)}, u32[]{:S(2)}, u32[]{:S(2)}) %all-to-all-start.7) | async-done | bytes 131104 | tf_op jit(solution)/shard_map/all_to_all | solution.py:39
  170.2 8.1 %all-to-all-done.8 = bf16[8,64,128]{2,1,0:T(8,128)(2,1)S(1)} async-done(((bf16[8,64,128]{2,1,0:T(8,128)(2,1)}), bf16[8,64,128]{2,1,0:T(8,128)(2,1)S(1)}, u32[]{:S(2)}, u32[]{:S(2)}) %all-to-all-start.8) | async-done | bytes 131104 | tf_op jit(solution)/shard_map/all_to_all | solution.py:32
  179.1 5.8 %all-to-all-start.9 = ((bf16[8,64,128]{2,0,1:T(8,128)(2,1)}), bf16[8,64,128]{2,0,1:T(8,128)(2,1)S(1)}, u32[]{:S(2)}, u32[]{:S(2)}) async-start(bf16[8,64,128]{2,0,1:T(8,128)(2,1)} %copy.115), calls=%async_computation.9 | async-start | bytes 262144 | tf_op jit(solution)/shard_map/all_to_all | solution.py:31
  185.0 11.3 %all-to-all-done.9 = bf16[8,64,128]{2,0,1:T(8,128)(2,1)S(1)} async-done(((bf16[8,64,128]{2,0,1:T(8,128)(2,1)}), bf16[8,64,128]{2,0,1:T(8,128)(2,1)S(1)}, u32[]{:S(2)}, u32[]{:S(2)}) %all-to-all-start.9) | async-done | bytes 131104 | tf_op jit(solution)/shard_map/all_to_all | solution.py:31
  197.8 10.7 %all_to_all.81 = bf16[8,64,128]{2,1,0:T(8,128)(2,1)S(1)} all-to-all(bf16[8,64,128]{2,1,0:T(8,128)(2,1)S(1)} %bitcast.165), channel_id=1, replica_groups=mesh['region'=8,'sub'=64] {'region'}, dimensions={0} | all-to-all | bytes 262144 | tf_op jit(solution)/shard_map/all_to_all | solution.py:40
  209.2 5.8 %all-to-all-start.11 = ((bf16[8,64,128]{2,0,1:T(8,128)(2,1)}), bf16[8,64,128]{2,0,1:T(8,128)(2,1)S(1)}, u32[]{:S(2)}, u32[]{:S(2)}) async-start(bf16[8,64,128]{2,0,1:T(8,128)(2,1)} %copy.117), calls=%async_computation.11 | async-start | bytes 262144 | tf_op jit(solution)/shard_map/all_to_all | solution.py:39
  215.0 11.3 %all-to-all-done.11 = bf16[8,64,128]{2,0,1:T(8,128)(2,1)S(1)} async-done(((bf16[8,64,128]{2,0,1:T(8,128)(2,1)}), bf16[8,64,128]{2,0,1:T(8,128)(2,1)S(1)}, u32[]{:S(2)}, u32[]{:S(2)}) %all-to-all-start.11) | async-done | bytes 131104 | tf_op jit(solution)/shard_map/all_to_all | solution.py:39
  238.7 8.1 %all-to-all-done.12 = bf16[8,64,128]{2,1,0:T(8,128)(2,1)S(1)} async-done(((bf16[8,64,128]{2,1,0:T(8,128)(2,1)}), bf16[8,64,128]{2,1,0:T(8,128)(2,1)S(1)}, u32[]{:S(2)}, u32[]{:S(2)}) %all-to-all-start.12) | async-done | bytes 131104 | tf_op jit(solution)/shard_map/all_to_all | solution.py:32
  247.5 5.8 %all-to-all-start.13 = ((bf16[8,64,128]{2,0,1:T(8,128)(2,1)}), bf16[8,64,128]{2,0,1:T(8,128)(2,1)S(1)}, u32[]{:S(2)}, u32[]{:S(2)}) async-start(bf16[8,64,128]{2,0,1:T(8,128)(2,1)} %copy.122), calls=%async_computation.13 | async-start | bytes 262144 | tf_op jit(solution)/shard_map/all_to_all | solution.py:31
  253.5 11.2 %all-to-all-done.13 = bf16[8,64,128]{2,0,1:T(8,128)(2,1)S(1)} async-done(((bf16[8,64,128]{2,0,1:T(8,128)(2,1)}), bf16[8,64,128]{2,0,1:T(8,128)(2,1)S(1)}, u32[]{:S(2)}, u32[]{:S(2)}) %all-to-all-start.13) | async-done | bytes 131104 | tf_op jit(solution)/shard_map/all_to_all | solution.py:31
  266.2 10.7 %all_to_all.82 = bf16[8,64,128]{2,1,0:T(8,128)(2,1)S(1)} all-to-all(bf16[8,64,128]{2,1,0:T(8,128)(2,1)S(1)} %bitcast.166), channel_id=1, replica_groups=mesh['region'=8,'sub'=64] {'region'}, dimensions={0} | all-to-all | bytes 262144 | tf_op jit(solution)/shard_map/all_to_all | solution.py:40
  277.0 16.3 %all_to_all.83 = bf16[8,64,128]{2,0,1:T(8,128)(2,1)S(1)} all-to-all(bf16[8,64,128]{2,0,1:T(8,128)(2,1)S(1)} %copy.124), channel_id=1, replica_groups=mesh['region'=8,'sub'=64] {'sub'}, dimensions={1} | all-to-all | bytes 262144 | tf_op jit(solution)/shard_map/all_to_all | solution.py:39
  299.9 72.5 %all-gather.2.cloned.1.call-done = bf16[4096,256]{1,0:T(8,128)(2,1)} async-done(((bf16[64,256]{1,0:T(8,128)(2,1)}), bf16[4096,256]{1,0:T(8,128)(2,1)}) %all-gather.2.cloned.1.call-update) | async-done | bytes 2097168 | tf_op jit(solution)/shard_map/all_gather | solution.py:74
  (103 shorter events, 78.0 us)
Async XLA Ops:
  6.5 83.8 %copy-start = (bf16[1,1,1024,1024]{3,2,1,0:T(8,128)(2,1)S(1)}, bf16[1,1,1024,1024]{3,2,1,0:T(8,128)(2,1)}, u32[]{:S(2)}) copy-start(bf16[1,1,1024,1024]{3,2,1,0:T(8,128)(2,1)} %param.12) | copy-start | bytes 6291460
  6.5 16.7 %copy-start.3 = (s32[4,512]{1,0:T(4,128)S(1)}, s32[4,512]{1,0:T(4,128)}, u32[]{:S(2)}) copy-start(s32[4,512]{1,0:T(4,128)} %param.15) | copy-start | bytes 24580
  12.3 18.6 %all-to-all-start = ((bf16[8,64,128]{2,1,0:T(8,128)(2,1)}), bf16[8,64,128]{2,1,0:T(8,128)(2,1)S(1)}, u32[]{:S(2)}, u32[]{:S(2)}) async-start(bf16[8,64,128]{2,1,0:T(8,128)(2,1)} %convert_element_type.77), calls=%async_computation | async-start | bytes 262144 | tf_op jit(solution)/shard_map/all_to_all | solution.py:32
  31.7 23.5 %all-to-all-start.1 = ((bf16[8,64,128]{2,0,1:T(8,128)(2,1)}), bf16[8,64,128]{2,0,1:T(8,128)(2,1)S(1)}, u32[]{:S(2)}, u32[]{:S(2)}) async-start(bf16[8,64,128]{2,0,1:T(8,128)(2,1)} %copy.98), calls=%async_computation.1 | async-start | bytes 262144 | tf_op jit(solution)/shard_map/all_to_all | solution.py:31
  68.2 17.1 %all-to-all-start.3 = ((bf16[8,64,128]{2,0,1:T(8,128)(2,1)}), bf16[8,64,128]{2,0,1:T(8,128)(2,1)S(1)}, u32[]{:S(2)}, u32[]{:S(2)}) async-start(bf16[8,64,128]{2,0,1:T(8,128)(2,1)} %copy.100), calls=%async_computation.3 | async-start | bytes 262144 | tf_op jit(solution)/shard_map/all_to_all | solution.py:39
  97.0 11.5 %all-to-all-start.4 = ((bf16[8,64,128]{2,1,0:T(8,128)(2,1)}), bf16[8,64,128]{2,1,0:T(8,128)(2,1)S(1)}, u32[]{:S(2)}, u32[]{:S(2)}) async-start(bf16[8,64,128]{2,1,0:T(8,128)(2,1)} %convert_element_type.83), calls=%async_computation.4 | async-start | bytes 262144 | tf_op jit(solution)/shard_map/all_to_all | solution.py:32
  109.3 17.2 %all-to-all-start.5 = ((bf16[8,64,128]{2,0,1:T(8,128)(2,1)}), bf16[8,64,128]{2,0,1:T(8,128)(2,1)S(1)}, u32[]{:S(2)}, u32[]{:S(2)}) async-start(bf16[8,64,128]{2,0,1:T(8,128)(2,1)} %copy.108), calls=%async_computation.5 | async-start | bytes 262144 | tf_op jit(solution)/shard_map/all_to_all | solution.py:31
  128.6 11.5 %all-to-all-start.6 = ((bf16[8,64,128]{2,1,0:T(8,128)(2,1)}), bf16[8,64,128]{2,1,0:T(8,128)(2,1)S(1)}, u32[]{:S(2)}, u32[]{:S(2)}) async-start(bf16[8,64,128]{2,1,0:T(8,128)(2,1)} %bitcast.17), calls=%async_computation.6 | async-start | bytes 262144 | tf_op jit(solution)/shard_map/all_to_all | solution.py:40
  140.9 17.2 %all-to-all-start.7 = ((bf16[8,64,128]{2,0,1:T(8,128)(2,1)}), bf16[8,64,128]{2,0,1:T(8,128)(2,1)S(1)}, u32[]{:S(2)}, u32[]{:S(2)}) async-start(bf16[8,64,128]{2,0,1:T(8,128)(2,1)} %copy.110), calls=%async_computation.7 | async-start | bytes 262144 | tf_op jit(solution)/shard_map/all_to_all | solution.py:39
  166.8 11.5 %all-to-all-start.8 = ((bf16[8,64,128]{2,1,0:T(8,128)(2,1)}), bf16[8,64,128]{2,1,0:T(8,128)(2,1)S(1)}, u32[]{:S(2)}, u32[]{:S(2)}) async-start(bf16[8,64,128]{2,1,0:T(8,128)(2,1)} %convert_element_type.86), calls=%async_computation.8 | async-start | bytes 262144 | tf_op jit(solution)/shard_map/all_to_all | solution.py:32
  179.1 17.2 %all-to-all-start.9 = ((bf16[8,64,128]{2,0,1:T(8,128)(2,1)}), bf16[8,64,128]{2,0,1:T(8,128)(2,1)S(1)}, u32[]{:S(2)}, u32[]{:S(2)}) async-start(bf16[8,64,128]{2,0,1:T(8,128)(2,1)} %copy.115), calls=%async_computation.9 | async-start | bytes 262144 | tf_op jit(solution)/shard_map/all_to_all | solution.py:31
  209.2 17.1 %all-to-all-start.11 = ((bf16[8,64,128]{2,0,1:T(8,128)(2,1)}), bf16[8,64,128]{2,0,1:T(8,128)(2,1)S(1)}, u32[]{:S(2)}, u32[]{:S(2)}) async-start(bf16[8,64,128]{2,0,1:T(8,128)(2,1)} %copy.117), calls=%async_computation.11 | async-start | bytes 262144 | tf_op jit(solution)/shard_map/all_to_all | solution.py:39
  235.3 11.5 %all-to-all-start.12 = ((bf16[8,64,128]{2,1,0:T(8,128)(2,1)}), bf16[8,64,128]{2,1,0:T(8,128)(2,1)S(1)}, u32[]{:S(2)}, u32[]{:S(2)}) async-start(bf16[8,64,128]{2,1,0:T(8,128)(2,1)} %convert_element_type.89), calls=%async_computation.12 | async-start | bytes 262144 | tf_op jit(solution)/shard_map/all_to_all | solution.py:32
  247.5 17.2 %all-to-all-start.13 = ((bf16[8,64,128]{2,0,1:T(8,128)(2,1)}), bf16[8,64,128]{2,0,1:T(8,128)(2,1)S(1)}, u32[]{:S(2)}, u32[]{:S(2)}) async-start(bf16[8,64,128]{2,0,1:T(8,128)(2,1)} %copy.122), calls=%async_computation.13 | async-start | bytes 262144 | tf_op jit(solution)/shard_map/all_to_all | solution.py:31
  253.4 119.0 %all-gather.2.cloned.1.call-start = ((), (), s32[]{:S(2)}) async-start(), calls=%async_computation.16 | async-start | bytes 2129920 | tf_op jit(solution)/shard_map/all_gather | solution.py:74
  297.0 1.8 copy-start.2
  297.8 1.0 copy-start.1
Sparse Core Ops, SparseCore 0:
  300.1 72.3 all-gather.1
where the time goes:
time: 386 us; the launch traced here: 384 us
  waiting for transfers between devices  192 us (50%)
  starting transfers between devices  71.6 us (19%)
  blocking collectives  48.4 us (13%)
  local copies, waits for them, and re-layouts  32.8 us (8%)
  matrix products  24.2 us (6%)
  between operations  13.9 us (4%)
    all_gather x1, waiting for transfers between devices, shards(): lax.all_gather(projected, 'sub', axis=0, tiled=True)  72.5 us
    all_to_all x4, waiting for transfers between devices, shards(): lax.all_to_all(lax.all_to_all(pieces, 'region', split_axis=0, concat_axis...  44.9 us
    all_to_all x3, waiting for transfers between devices, shards(): lax.all_to_all(lax.all_to_all(relayed.reshape(region_peers, sub_peers, pi...  33.9 us
    all_to_all x4, waiting for transfers between devices, shards(): lax.all_to_all(pieces, 'region', split_axis=0, concat_axis=0, tiled=True)  32.1 us
    all_to_all x3, blocking collectives, shards(): lax.all_to_all(relayed.reshape(region_peers, sub_peers, piece_len), 'regi...  32.1 us
    all_to_all x4, starting transfers between devices, shards(): lax.all_to_all(lax.all_to_all(pieces, 'region', split_axis=0, concat_axis...  29.9 us
    all_to_all x4, starting transfers between devices, shards(): lax.all_to_all(pieces, 'region', split_axis=0, concat_axis=0, tiled=True)  21 us
    all_to_all x3, starting transfers between devices, shards(): lax.all_to_all(lax.all_to_all(relayed.reshape(region_peers, sub_peers, pi...  17.3 us
  transfers between devices with their start and end apart: 13, of which 13 were waited for; matrix products, arithmetic and copies ran while one was open for 0% of the time, Pallas kernels for 0%

commit v1 on v0

--- a/solution.py
+++ b/solution.py
@@ -9,6 +9,13 @@
 
 
 def shards(right_side, local_inverse, coupling, margin_blocks, partner, restriction, coarse_rows):
+
+    def _build_region(shard_in, named_axis):
+        return jnp.concatenate(
+            lax.all_to_all(jnp.stack(lax.psum(1, named_axis) * [shard_in]), named_axis, 0, 0),
+            axis=0,
+        )
+
     inverse = local_inverse[0, 0]
     tile_set = coupling[0, 0]
     own_blocks = margin_blocks[:, 0, 0, :]
@@ -70,9 +77,7 @@
     )
     own_rows = coarse_rows[0]
     coarse = jnp.dot(
-        own_rows,
-        lax.all_gather(projected, "sub", axis=0, tiled=True),
-        preferred_element_type=jnp.float32,
+        own_rows, _build_region(projected, "sub"), preferred_element_type=jnp.float32
     ).astype(jnp.bfloat16)
     lifted = lax.dot_general(
         own_restriction, coarse, (((0,), (0,)), ((), ())), preferred_element_type=jnp.float32

time: 386 us -> 355 us (0.920)
  waiting for transfers between devices: 192 us -> 119 us
  blocking collectives: 48.4 us -> 103 us
  between operations: 13.9 us -> 0.53 us
    all_gather x1 -> x0, waiting for transfers between devices: 72.5 us -> none  [shards(): lax.all_gather(projected, 'sub', axis=0, tiled=True)]
    all_to_all x0 -> x1, blocking collectives: none -> 54.4 us  [_build_region(): lax.all_to_all(jnp.stack(lax.psum(1, named_axis) * [shard_in]), named_axi...]
  transfers between devices with their start and end apart: 13 -> 12, of which waited for: 13 -> 12; matrix products, arithmetic and copies ran while one was open for 0% -> 0% of each run, Pallas kernels for 0% -> 0%
where the time goes in v1:
time: 355 us; the launch traced here: 353 us
  waiting for transfers between devices  119 us (34%)
  blocking collectives  103 us (29%)
  starting transfers between devices  71.6 us (20%)
  local copies, waits for them, and re-layouts  33.5 us (9%)
  matrix products  24.1 us (7%)
    all_to_all x1, blocking collectives, _build_region(): lax.all_to_all(jnp.stack(lax.psum(1, named_axis) * [shard_in]), named_axi...  54.4 us
    all_to_all x4, waiting for transfers between devices, shards(): lax.all_to_all(lax.all_to_all(pieces, 'region', split_axis=0, concat_axis...  45 us
    all_to_all x3, waiting for transfers between devices, shards(): lax.all_to_all(lax.all_to_all(relayed.reshape(region_peers, sub_peers, pi...  33.9 us
    all_to_all x4, waiting for transfers between devices, shards(): lax.all_to_all(pieces, 'region', split_axis=0, concat_axis=0, tiled=True)  32.1 us
    all_to_all x3, blocking collectives, shards(): lax.all_to_all(relayed.reshape(region_peers, sub_peers, piece_len), 'regi...  32.1 us
    all_to_all x4, starting transfers between devices, shards(): lax.all_to_all(lax.all_to_all(pieces, 'region', split_axis=0, concat_axis...  29.9 us
    all_to_all x4, starting transfers between devices, shards(): lax.all_to_all(pieces, 'region', split_axis=0, concat_axis=0, tiled=True)  21 us
    all_to_all x3, starting transfers between devices, shards(): lax.all_to_all(lax.all_to_all(relayed.reshape(region_peers, sub_peers, pi...  17.3 us
  transfers between devices with their start and end apart: 12, of which 12 were waited for; matrix products, arithmetic and copies ran while one was open for 0% of the time, Pallas kernels for 0%

profile of v1, /device:TPU:1, one launch (start us, length us, event | category | flops | bytes accessed | tf_op | source)
XLA Modules:
  0.0 353.4 jit_solution(14177012602061867764)
XLA Ops:
  5.8 10.9 %all-to-all-start = ((bf16[8,64,128]{2,1,0:T(8,128)(2,1)}), bf16[8,64,128]{2,1,0:T(8,128)(2,1)S(1)}, u32[]{:S(2)}, u32[]{:S(2)}) async-start(bf16[8,64,128]{2,1,0:T(8,128)(2,1)} %convert_element_type.77), calls=%async_computation | async-start | bytes 262144 | tf_op jit(solution)/shard_map/all_to_all | solution.py:39
  16.7 7.7 %all-to-all-done = bf16[8,64,128]{2,1,0:T(8,128)(2,1)S(1)} async-done(((bf16[8,64,128]{2,1,0:T(8,128)(2,1)}), bf16[8,64,128]{2,1,0:T(8,128)(2,1)S(1)}, u32[]{:S(2)}, u32[]{:S(2)}) %all-to-all-start) | async-done | bytes 131104 | tf_op jit(solution)/shard_map/all_to_all | solution.py:39
  25.1 12.4 %all-to-all-start.1 = ((bf16[8,64,128]{2,0,1:T(8,128)(2,1)}), bf16[8,64,128]{2,0,1:T(8,128)(2,1)S(1)}, u32[]{:S(2)}, u32[]{:S(2)}) async-start(bf16[8,64,128]{2,0,1:T(8,128)(2,1)} %copy.98), calls=%async_computation.1 | async-start | bytes 262144 | tf_op jit(solution)/shard_map/all_to_all | solution.py:38
  37.6 11.1 %all-to-all-done.1 = bf16[8,64,128]{2,0,1:T(8,128)(2,1)S(1)} async-done(((bf16[8,64,128]{2,0,1:T(8,128)(2,1)}), bf16[8,64,128]{2,0,1:T(8,128)(2,1)S(1)}, u32[]{:S(2)}, u32[]{:S(2)}) %all-to-all-start.1) | async-done | bytes 131104 | tf_op jit(solution)/shard_map/all_to_all | solution.py:38
  50.2 10.7 %all_to_all.85 = bf16[8,64,128]{2,1,0:T(8,128)(2,1)S(1)} all-to-all(bf16[8,64,128]{2,1,0:T(8,128)(2,1)S(1)} %bitcast.166), channel_id=1, replica_groups=mesh['region'=8,'sub'=64] {'region'}, dimensions={0} | all-to-all | bytes 262144 | tf_op jit(solution)/shard_map/all_to_all | solution.py:47
  67.4 11.3 %all-to-all-done.3 = bf16[8,64,128]{2,0,1:T(8,128)(2,1)S(1)} async-done(((bf16[8,64,128]{2,0,1:T(8,128)(2,1)}), bf16[8,64,128]{2,0,1:T(8,128)(2,1)S(1)}, u32[]{:S(2)}, u32[]{:S(2)}) %all-to-all-start.3) | async-done | bytes 131104 | tf_op jit(solution)/shard_map/all_to_all | solution.py:46
  93.8 8.1 %all-to-all-done.4 = bf16[8,64,128]{2,1,0:T(8,128)(2,1)S(1)} async-done(((bf16[8,64,128]{2,1,0:T(8,128)(2,1)}), bf16[8,64,128]{2,1,0:T(8,128)(2,1)S(1)}, u32[]{:S(2)}, u32[]{:S(2)}) %all-to-all-start.4) | async-done | bytes 131104 | tf_op jit(solution)/shard_map/all_to_all | solution.py:39
  102.7 5.8 %all-to-all-start.5 = ((bf16[8,64,128]{2,0,1:T(8,128)(2,1)}), bf16[8,64,128]{2,0,1:T(8,128)(2,1)S(1)}, u32[]{:S(2)}, u32[]{:S(2)}) async-start(bf16[8,64,128]{2,0,1:T(8,128)(2,1)} %copy.108), calls=%async_computation.5 | async-start | bytes 262144 | tf_op jit(solution)/shard_map/all_to_all | solution.py:38
  108.6 11.3 %all-to-all-done.5 = bf16[8,64,128]{2,0,1:T(8,128)(2,1)S(1)} async-done(((bf16[8,64,128]{2,0,1:T(8,128)(2,1)}), bf16[8,64,128]{2,0,1:T(8,128)(2,1)S(1)}, u32[]{:S(2)}, u32[]{:S(2)}) %all-to-all-start.5) | async-done | bytes 131104 | tf_op jit(solution)/shard_map/all_to_all | solution.py:38
  125.5 8.1 %all-to-all-done.6 = bf16[8,64,128]{2,1,0:T(8,128)(2,1)S(1)} async-done(((bf16[8,64,128]{2,1,0:T(8,128)(2,1)}), bf16[8,64,128]{2,1,0:T(8,128)(2,1)S(1)}, u32[]{:S(2)}, u32[]{:S(2)}) %all-to-all-start.6) | async-done | bytes 131104 | tf_op jit(solution)/shard_map/all_to_all | solution.py:47
  134.3 5.8 %all-to-all-start.7 = ((bf16[8,64,128]{2,0,1:T(8,128)(2,1)}), bf16[8,64,128]{2,0,1:T(8,128)(2,1)S(1)}, u32[]{:S(2)}, u32[]{:S(2)}) async-start(bf16[8,64,128]{2,0,1:T(8,128)(2,1)} %copy.110), calls=%async_computation.7 | async-start | bytes 262144 | tf_op jit(solution)/shard_map/all_to_all | solution.py:46
  140.2 11.3 %all-to-all-done.7 = bf16[8,64,128]{2,0,1:T(8,128)(2,1)S(1)} async-done(((bf16[8,64,128]{2,0,1:T(8,128)(2,1)}), bf16[8,64,128]{2,0,1:T(8,128)(2,1)S(1)}, u32[]{:S(2)}, u32[]{:S(2)}) %all-to-all-start.7) | async-done | bytes 131104 | tf_op jit(solution)/shard_map/all_to_all | solution.py:46
  163.7 8.1 %all-to-all-done.8 = bf16[8,64,128]{2,1,0:T(8,128)(2,1)S(1)} async-done(((bf16[8,64,128]{2,1,0:T(8,128)(2,1)}), bf16[8,64,128]{2,1,0:T(8,128)(2,1)S(1)}, u32[]{:S(2)}, u32[]{:S(2)}) %all-to-all-start.8) | async-done | bytes 131104 | tf_op jit(solution)/shard_map/all_to_all | solution.py:39
  172.6 5.8 %all-to-all-start.9 = ((bf16[8,64,128]{2,0,1:T(8,128)(2,1)}), bf16[8,64,128]{2,0,1:T(8,128)(2,1)S(1)}, u32[]{:S(2)}, u32[]{:S(2)}) async-start(bf16[8,64,128]{2,0,1:T(8,128)(2,1)} %copy.115), calls=%async_computation.9 | async-start | bytes 262144 | tf_op jit(solution)/shard_map/all_to_all | solution.py:38
  178.5 11.3 %all-to-all-done.9 = bf16[8,64,128]{2,0,1:T(8,128)(2,1)S(1)} async-done(((bf16[8,64,128]{2,0,1:T(8,128)(2,1)}), bf16[8,64,128]{2,0,1:T(8,128)(2,1)S(1)}, u32[]{:S(2)}, u32[]{:S(2)}) %all-to-all-start.9) | async-done | bytes 131104 | tf_op jit(solution)/shard_map/all_to_all | solution.py:38
  191.3 10.7 %all_to_all.86 = bf16[8,64,128]{2,1,0:T(8,128)(2,1)S(1)} all-to-all(bf16[8,64,128]{2,1,0:T(8,128)(2,1)S(1)} %bitcast.167), channel_id=1, replica_groups=mesh['region'=8,'sub'=64] {'region'}, dimensions={0} | all-to-all | bytes 262144 | tf_op jit(solution)/shard_map/all_to_all | solution.py:47
  202.7 5.8 %all-to-all-start.11 = ((bf16[8,64,128]{2,0,1:T(8,128)(2,1)}), bf16[8,64,128]{2,0,1:T(8,128)(2,1)S(1)}, u32[]{:S(2)}, u32[]{:S(2)}) async-start(bf16[8,64,128]{2,0,1:T(8,128)(2,1)} %copy.117), calls=%async_computation.11 | async-start | bytes 262144 | tf_op jit(solution)/shard_map/all_to_all | solution.py:46
  208.5 11.3 %all-to-all-done.11 = bf16[8,64,128]{2,0,1:T(8,128)(2,1)S(1)} async-done(((bf16[8,64,128]{2,0,1:T(8,128)(2,1)}), bf16[8,64,128]{2,0,1:T(8,128)(2,1)S(1)}, u32[]{:S(2)}, u32[]{:S(2)}) %all-to-all-start.11) | async-done | bytes 131104 | tf_op jit(solution)/shard_map/all_to_all | solution.py:46
  232.2 8.1 %all-to-all-done.12 = bf16[8,64,128]{2,1,0:T(8,128)(2,1)S(1)} async-done(((bf16[8,64,128]{2,1,0:T(8,128)(2,1)}), bf16[8,64,128]{2,1,0:T(8,128)(2,1)S(1)}, u32[]{:S(2)}, u32[]{:S(2)}) %all-to-all-start.12) | async-done | bytes 131104 | tf_op jit(solution)/shard_map/all_to_all | solution.py:39
  241.0 5.8 %all-to-all-start.13 = ((bf16[8,64,128]{2,0,1:T(8,128)(2,1)}), bf16[8,64,128]{2,0,1:T(8,128)(2,1)S(1)}, u32[]{:S(2)}, u32[]{:S(2)}) async-start(bf16[8,64,128]{2,0,1:T(8,128)(2,1)} %copy.122), calls=%async_computation.13 | async-start | bytes 262144 | tf_op jit(solution)/shard_map/all_to_all | solution.py:38
  246.9 11.3 %all-to-all-done.13 = bf16[8,64,128]{2,0,1:T(8,128)(2,1)S(1)} async-done(((bf16[8,64,128]{2,0,1:T(8,128)(2,1)}), bf16[8,64,128]{2,0,1:T(8,128)(2,1)S(1)}, u32[]{:S(2)}, u32[]{:S(2)}) %all-to-all-start.13) | async-done | bytes 131104 | tf_op jit(solution)/shard_map/all_to_all | solution.py:38
  259.7 10.7 %all_to_all.87 = bf16[8,64,128]{2,1,0:T(8,128)(2,1)S(1)} all-to-all(bf16[8,64,128]{2,1,0:T(8,128)(2,1)S(1)} %bitcast.168), channel_id=1, replica_groups=mesh['region'=8,'sub'=64] {'region'}, dimensions={0} | all-to-all | bytes 262144 | tf_op jit(solution)/shard_map/all_to_all | solution.py:47
  270.5 16.3 %all_to_all.88 = bf16[8,64,128]{2,0,1:T(8,128)(2,1)S(1)} all-to-all(bf16[8,64,128]{2,0,1:T(8,128)(2,1)S(1)} %copy.124), channel_id=1, replica_groups=mesh['region'=8,'sub'=64] {'sub'}, dimensions={1} | all-to-all | bytes 262144 | tf_op jit(solution)/shard_map/all_to_all | solution.py:46
  292.4 54.4 %all_to_all.89 = bf16[64,64,256]{2,1,0:T(8,128)(2,1)} all-to-all(bf16[64,64,256]{2,1,0:T(8,128)(2,1)S(1)} %stack.2), channel_id=1, replica_groups=mesh['region'=8,'sub'=64] {'sub'}, dimensions={0} | all-to-all | bytes 4194304 | tf_op jit(solution)/shard_map/all_to_all | solution.py:15
  (104 shorter events, 78.6 us)
Async XLA Ops:
  0.0 83.8 %copy-start = (bf16[1,1,1024,1024]{3,2,1,0:T(8,128)(2,1)S(1)}, bf16[1,1,1024,1024]{3,2,1,0:T(8,128)(2,1)}, u32[]{:S(2)}) copy-start(bf16[1,1,1024,1024]{3,2,1,0:T(8,128)(2,1)} %param.12) | copy-start | bytes 6291460
  0.0 16.7 %copy-start.4 = (s32[4,512]{1,0:T(4,128)S(1)}, s32[4,512]{1,0:T(4,128)}, u32[]{:S(2)}) copy-start(s32[4,512]{1,0:T(4,128)} %param.15) | copy-start | bytes 24580
  5.8 18.6 %all-to-all-start = ((bf16[8,64,128]{2,1,0:T(8,128)(2,1)}), bf16[8,64,128]{2,1,0:T(8,128)(2,1)S(1)}, u32[]{:S(2)}, u32[]{:S(2)}) async-start(bf16[8,64,128]{2,1,0:T(8,128)(2,1)} %convert_element_type.77), calls=%async_computation | async-start | bytes 262144 | tf_op jit(solution)/shard_map/all_to_all | solution.py:39
  25.1 23.5 %all-to-all-start.1 = ((bf16[8,64,128]{2,0,1:T(8,128)(2,1)}), bf16[8,64,128]{2,0,1:T(8,128)(2,1)S(1)}, u32[]{:S(2)}, u32[]{:S(2)}) async-start(bf16[8,64,128]{2,0,1:T(8,128)(2,1)} %copy.98), calls=%async_computation.1 | async-start | bytes 262144 | tf_op jit(solution)/shard_map/all_to_all | solution.py:38
  61.6 17.1 %all-to-all-start.3 = ((bf16[8,64,128]{2,0,1:T(8,128)(2,1)}), bf16[8,64,128]{2,0,1:T(8,128)(2,1)S(1)}, u32[]{:S(2)}, u32[]{:S(2)}) async-start(bf16[8,64,128]{2,0,1:T(8,128)(2,1)} %copy.100), calls=%async_computation.3 | async-start | bytes 262144 | tf_op jit(solution)/shard_map/all_to_all | solution.py:46
  90.5 11.5 %all-to-all-start.4 = ((bf16[8,64,128]{2,1,0:T(8,128)(2,1)}), bf16[8,64,128]{2,1,0:T(8,128)(2,1)S(1)}, u32[]{:S(2)}, u32[]{:S(2)}) async-start(bf16[8,64,128]{2,1,0:T(8,128)(2,1)} %convert_element_type.83), calls=%async_computation.4 | async-start | bytes 262144 | tf_op jit(solution)/shard_map/all_to_all | solution.py:39
  102.7 17.2 %all-to-all-start.5 = ((bf16[8,64,128]{2,0,1:T(8,128)(2,1)}), bf16[8,64,128]{2,0,1:T(8,128)(2,1)S(1)}, u32[]{:S(2)}, u32[]{:S(2)}) async-start(bf16[8,64,128]{2,0,1:T(8,128)(2,1)} %copy.108), calls=%async_computation.5 | async-start | bytes 262144 | tf_op jit(solution)/shard_map/all_to_all | solution.py:38
  122.1 11.5 %all-to-all-start.6 = ((bf16[8,64,128]{2,1,0:T(8,128)(2,1)}), bf16[8,64,128]{2,1,0:T(8,128)(2,1)S(1)}, u32[]{:S(2)}, u32[]{:S(2)}) async-start(bf16[8,64,128]{2,1,0:T(8,128)(2,1)} %bitcast.17), calls=%async_computation.6 | async-start | bytes 262144 | tf_op jit(solution)/shard_map/all_to_all | solution.py:47
  134.3 17.2 %all-to-all-start.7 = ((bf16[8,64,128]{2,0,1:T(8,128)(2,1)}), bf16[8,64,128]{2,0,1:T(8,128)(2,1)S(1)}, u32[]{:S(2)}, u32[]{:S(2)}) async-start(bf16[8,64,128]{2,0,1:T(8,128)(2,1)} %copy.110), calls=%async_computation.7 | async-start | bytes 262144 | tf_op jit(solution)/shard_map/all_to_all | solution.py:46
  160.3 11.5 %all-to-all-start.8 = ((bf16[8,64,128]{2,1,0:T(8,128)(2,1)}), bf16[8,64,128]{2,1,0:T(8,128)(2,1)S(1)}, u32[]{:S(2)}, u32[]{:S(2)}) async-start(bf16[8,64,128]{2,1,0:T(8,128)(2,1)} %convert_element_type.86), calls=%async_computation.8 | async-start | bytes 262144 | tf_op jit(solution)/shard_map/all_to_all | solution.py:39
  172.6 17.2 %all-to-all-start.9 = ((bf16[8,64,128]{2,0,1:T(8,128)(2,1)}), bf16[8,64,128]{2,0,1:T(8,128)(2,1)S(1)}, u32[]{:S(2)}, u32[]{:S(2)}) async-start(bf16[8,64,128]{2,0,1:T(8,128)(2,1)} %copy.115), calls=%async_computation.9 | async-start | bytes 262144 | tf_op jit(solution)/shard_map/all_to_all | solution.py:38
  202.7 17.1 %all-to-all-start.11 = ((bf16[8,64,128]{2,0,1:T(8,128)(2,1)}), bf16[8,64,128]{2,0,1:T(8,128)(2,1)S(1)}, u32[]{:S(2)}, u32[]{:S(2)}) async-start(bf16[8,64,128]{2,0,1:T(8,128)(2,1)} %copy.117), calls=%async_computation.11 | async-start | bytes 262144 | tf_op jit(solution)/shard_map/all_to_all | solution.py:46
  228.8 11.5 %all-to-all-start.12 = ((bf16[8,64,128]{2,1,0:T(8,128)(2,1)}), bf16[8,64,128]{2,1,0:T(8,128)(2,1)S(1)}, u32[]{:S(2)}, u32[]{:S(2)}) async-start(bf16[8,64,128]{2,1,0:T(8,128)(2,1)} %convert_element_type.89), calls=%async_computation.12 | async-start | bytes 262144 | tf_op jit(solution)/shard_map/all_to_all | solution.py:39
  241.0 17.2 %all-to-all-start.13 = ((bf16[8,64,128]{2,0,1:T(8,128)(2,1)}), bf16[8,64,128]{2,0,1:T(8,128)(2,1)S(1)}, u32[]{:S(2)}, u32[]{:S(2)}) async-start(bf16[8,64,128]{2,0,1:T(8,128)(2,1)} %copy.122), calls=%async_computation.13 | async-start | bytes 262144 | tf_op jit(solution)/shard_map/all_to_all | solution.py:38
  290.5 0.9 copy-start.3
  291.4 1.0 copy-start.1
  292.4 54.5 %copy-start.2 = (f32[256,1024]{1,0:T(8,128)S(1)}, f32[256,1024]{1,0:T(8,128)}, u32[]{:S(2)}) copy-start(f32[256,1024]{1,0:T(8,128)} %get-tuple-element.18) | copy-start | bytes 3145732
